TPU v7x, 512 devices: a whole 4x8x8 slice. The times are simulated.
512 devices in a mesh: seq: 128 (over z, y, core), tp: 4 (over x).
Axes of the slice: x: 4, y: 8, z: 8, core: 2. Of those that a mesh axis runs over, the one named last changes fastest.
Arguments:
- hidden_in: bfloat16 [16384, 1536], P('seq'), may hold values from -6 to 6
- w_query: bfloat16 [1536, 1536], P(None, 'tp'), may hold values from -0.625 to 0.625
- key_weight: bfloat16 [1536, 512], P(None, 'tp'), may hold values from -0.625 to 0.625
- value_weight: bfloat16 [1536, 512], P(None, 'tp'), may hold values from -0.15625 to 0.15625
- w_out: bfloat16 [1536, 1536], P('tp'), may hold values from -0.4375 to 0.4375
- cached_prefix_keys: bfloat16 [4096, 512], P('seq', 'tp'), may hold values from -60000 to 60000
- cached_prefix_values: bfloat16 [4096, 512], P('seq', 'tp'), may hold values from -6 to 6
- doc_ids: int32 [128, 128], P('seq'), may hold values from 0 to 3, never falling along the last dimension, each value on 1 to 64 neighbouring positions
- routes: int32 [16384, 8], P(('seq', 'tp')), may hold values from 0 to 31, all different within a row; in each aligned block of 32 rows (0 to 31, 32 to 63, ...) at most 16 rows name the same one
- gate_scores: float32 [16384, 8], P(('seq', 'tp')), may hold values from 0.2 to 1
- expert_in: bfloat16 [128, 1536, 256], P('seq'), may hold values from -0.15625 to 0.15625
- expert_out: bfloat16 [128, 128, 1536], P('seq'), may hold values from -0.25 to 0.25
Outputs:
- attn_proj: bfloat16 [16384, 1536], P(('seq', 'tp'))
- expert_mix: bfloat16 [16384, 1536], P(('seq', 'tp'))
- layer_out: bfloat16 [16384, 1536], P(('seq', 'tp'))
Inputs may be any that keep to these rules, and one draw needn't show every extreme that they name: `routes`: within the rows of one device (aligned blocks of 32 tokens) no expert is picked by more than 16 tokens, a bound that some block reaches; every expert is picked somewhere.
All inputs are finite; a program needn't handle non-finite values.
Results may differ from a plain program's by a relative error of at most 0.028.
Values may be sent and summed in bfloat16 or wider, within the bound.
No kernel may reach another device: no remote copies, remote signals or barrier semaphores. Data moves between devices by JAX's collectives and lax.ppermute only.
A program may use at most 64 MiB of HBM per device.

v0:
```python
import jax
import jax.numpy as jnp
from jax import lax
from jax.sharding import Mesh, PartitionSpec as P

HEAD_WIDTH = 64
EXPERTS = 32
SEQ = ("z", "yh", "yl", "c")
EXPERT_AXES = ("z", "yh")
PART_AXES = ("yl", "c")
EPSILON = 1e-06
RESIDUAL = 0.22


def normalize(values):
    values = values.astype(jnp.float32)
    return values * lax.rsqrt(jnp.mean(values * values, axis=-1, keepdims=True) + EPSILON)


def rotary_apply(values, token_positions):
    half_size = values.shape[-1] // 2
    frequency = jnp.exp(
        -jnp.log(10000.0) * jnp.arange(half_size, dtype=jnp.float32) * 2.0 / values.shape[-1]
    )
    angles = token_positions[:, None] * frequency[None, :]
    cosine = jnp.cos(angles)[:, None, :]
    sine_part = jnp.sin(angles)[:, None, :]
    first_half = values[..., :half_size]
    second = values[..., half_size:]
    return jnp.concatenate(
        [first_half * cosine - second * sine_part, second * cosine + first_half * sine_part],
        axis=-1,
    )


def body(
    hidden_in,
    w_query,
    key_weight,
    value_weight,
    w_out,
    cached_prefix_keys,
    cached_prefix_values,
    doc_ids,
    routes,
    gate_scores,
    expert_in,
    expert_out,
):
    rows_dev = hidden_in.shape[0]
    column_list = hidden_in.shape[1]
    head_size = HEAD_WIDTH
    kv_local = key_weight.shape[1] // head_size
    group_width = w_query.shape[1] // head_size // kv_local
    seq_count = lax.axis_size(SEQ)
    prefix_len = cached_prefix_keys.shape[0] * seq_count
    doc_row = doc_ids[0]
    row_index = jnp.arange(rows_dev, dtype=jnp.int32)
    same_doc = doc_row[:, None] == doc_row[None, :]
    doc_start = jnp.min(jnp.where(same_doc, row_index[None, :], rows_dev), axis=1)
    token_positions = (prefix_len + row_index - doc_start).astype(jnp.float32)
    normed_input = normalize(hidden_in).astype(jnp.bfloat16)
    query_rows_all = jnp.dot(normed_input, w_query, preferred_element_type=jnp.float32).reshape(
        rows_dev, kv_local * group_width, head_size
    )
    query_rows_all = (
        rotary_apply(query_rows_all, token_positions)
        .astype(jnp.bfloat16)
        .reshape(rows_dev, kv_local, group_width, head_size)
    )
    fresh_key = jnp.dot(normed_input, key_weight, preferred_element_type=jnp.float32).reshape(
        rows_dev, kv_local, head_size
    )
    fresh_key = rotary_apply(fresh_key, token_positions).astype(jnp.bfloat16)
    fresh_value = (
        jnp.dot(normed_input, value_weight, preferred_element_type=jnp.float32)
        .astype(jnp.bfloat16)
        .reshape(rows_dev, kv_local, head_size)
    )
    own_scores = (
        jnp.einsum("tkgd,skd->tkgs", query_rows_all, fresh_key, preferred_element_type=jnp.float32)
        / head_size
    )
    visible = same_doc & (row_index[None, :] <= row_index[:, None])
    own_scores = jnp.where(visible[:, None, None, :], own_scores, -jnp.inf)
    row_top = jnp.max(own_scores, axis=-1)
    weights = jnp.exp(own_scores - row_top[..., None])
    denominator = jnp.sum(weights, axis=-1)
    numerator = jnp.einsum(
        "tkgs,skd->tkgd",
        weights.astype(jnp.bfloat16),
        fresh_value,
        preferred_element_type=jnp.float32,
    )
    running = (row_top, denominator, numerator)
    prefix_both = jnp.concatenate([cached_prefix_keys, cached_prefix_values], axis=1)
    whole_both = lax.all_gather(prefix_both, SEQ, axis=0, tiled=True)
    kv_cols = cached_prefix_keys.shape[1]
    whole_keys = whole_both[:, :kv_cols]
    whole_values = whole_both[:, kv_cols:]
    top_old, denom_old, numer_old = running
    key_rows = whole_keys.reshape(-1, kv_local, head_size)
    value_rows = whole_values.reshape(-1, kv_local, head_size)
    scores = (
        jnp.einsum("tkgd,pkd->tkgp", query_rows_all, key_rows, preferred_element_type=jnp.float32)
        / head_size
    )
    top_new = jnp.maximum(top_old, jnp.max(scores, axis=-1))
    shrink = jnp.exp(top_old - top_new)
    part_weights = jnp.exp(scores - top_new[..., None])
    denom_new = denom_old * shrink + jnp.sum(part_weights, axis=-1)
    numer_new = numer_old * shrink[..., None] + jnp.einsum(
        "tkgp,pkd->tkgd",
        part_weights.astype(jnp.bfloat16),
        value_rows,
        preferred_element_type=jnp.float32,
    )
    running = (top_new, denom_new, numer_new)
    attended = (
        (running[2] / running[1][..., None])
        .astype(jnp.bfloat16)
        .reshape(rows_dev, kv_local * group_width * head_size)
    )
    moe_rows = routes.shape[0]
    row_start = lax.axis_index("tp") * moe_rows
    attn_sum = lax.psum_scatter(
        jnp.dot(attended, w_out, preferred_element_type=jnp.float32),
        "tp",
        scatter_dimension=0,
        tiled=True,
    )
    residual = (
        lax.dynamic_slice_in_dim(hidden_in, row_start, moe_rows, 0).astype(jnp.float32)
        + RESIDUAL * attn_sum
    )
    routed = normalize(residual).astype(jnp.bfloat16)
    experts = EXPERTS
    capacity = moe_rows // 2
    ff_part = expert_out.shape[1]
    onehot = (routes[:, :, None] == jnp.arange(experts, dtype=jnp.int32)[None, None, :]).astype(
        jnp.int32
    )
    per_row = jnp.sum(onehot, axis=1)
    before = jnp.cumsum(per_row, axis=0) - per_row
    rank_in = jnp.sum(onehot * before[:, None, :], axis=2)
    slot_of = routes * capacity + rank_in
    slot_ids = jnp.arange(experts * capacity, dtype=jnp.int32)
    pick_hit = slot_of[:, :, None] == slot_ids[None, None, :]
    selector = jnp.any(pick_hit, axis=1).T.astype(jnp.bfloat16)
    combiner = jnp.sum(jnp.where(pick_hit, gate_scores[:, :, None], 0.0), axis=1)
    gathered = jnp.dot(selector, routed, preferred_element_type=jnp.float32).astype(jnp.bfloat16)
    outgoing = gathered.reshape(experts, capacity, column_list)
    incoming = lax.all_to_all(outgoing, EXPERT_AXES, split_axis=0, concat_axis=0, tiled=True)
    incoming = incoming.reshape(experts * capacity, column_list)
    full_in = lax.all_gather(expert_in, PART_AXES, axis=0, tiled=True)
    full_out = lax.all_gather(expert_out, PART_AXES, axis=0, tiled=True)
    gate_up = jnp.einsum("rd,pdf->prf", incoming, full_in, preferred_element_type=jnp.float32)
    activated = (jax.nn.silu(gate_up[..., :ff_part]) * gate_up[..., ff_part:]).astype(jnp.bfloat16)
    partial_value = jnp.einsum(
        "prf,pfd->prd", activated, full_out, preferred_element_type=jnp.float32
    ).astype(jnp.bfloat16)
    part_total = jnp.sum(partial_value.astype(jnp.float32), axis=0).astype(jnp.bfloat16)
    returned = lax.all_to_all(
        part_total.reshape(experts, capacity, column_list),
        EXPERT_AXES,
        split_axis=0,
        concat_axis=0,
        tiled=True,
    )
    part_sum = returned.reshape(experts * capacity, column_list).astype(jnp.float32)
    expert_sum = jnp.dot(
        combiner, part_sum, precision=lax.Precision.HIGHEST, preferred_element_type=jnp.float32
    )
    layer_out = (residual + RESIDUAL * expert_sum).astype(jnp.bfloat16)
    return (attn_sum.astype(jnp.bfloat16), expert_sum.astype(jnp.bfloat16), layer_out)


def solution(mesh):
    seq_size = mesh.shape["seq"]
    tp_size = mesh.shape["tp"]
    split = (seq_size // 16, 4, 2, 2, tp_size)
    fine_mesh = Mesh(mesh.devices.reshape(split), ("z", "yh", "yl", "c", "tp"))
    seq_spec = SEQ
    in_specs = (
        P(seq_spec, None),
        P(None, "tp"),
        P(None, "tp"),
        P(None, "tp"),
        P("tp", None),
        P(seq_spec, "tp"),
        P(seq_spec, "tp"),
        P(seq_spec, None),
        P(SEQ + ("tp",), None),
        P(SEQ + ("tp",), None),
        P(seq_spec, None, None),
        P(seq_spec, None, None),
    )
    out_specs = (P(SEQ + ("tp",), None),) * 3
    return jax.shard_map(
        body, mesh=fine_mesh, in_specs=in_specs, out_specs=out_specs, check_vma=False
    )
```

profile of v0, /device:TPU:84, one launch (start us, length us, event | category | flops | bytes accessed | tf_op | source)
XLA Modules:
  0.0 280.1 jit_solution(2323323206248349324)
XLA Ops:
  8.1 1.4 pad_maximum_fusion.3
  9.6 0.8 fusion.25
  10.4 1.2 fusion.15
  11.6 0.8 compare_and_fusion
  12.6 1.5 fusion.37
  14.0 2.0 fusion.35
  16.1 0.3 fusion.41
  16.5 0.3 convolution_convert_fusion.1
  16.8 81.4 %all-gather.4.cloned.1.call-done = bf16[4096,256]{1,0:T(8,128)(2,1)} async-done(((bf16[32,256]{1,0:T(8,128)(2,1)}), bf16[4096,256]{1,0:T(8,128)(2,1)}) %all-gather.4.cloned.1.call-update) | async-done | bytes 2097168 | tf_op jit(solution)/shard_map/all_gather | solution.py:97
  98.2 3.0 %fusion.40 = (bf16[4096,128]{1,0:T(8,128)(2,1)}, bf16[4096,128]{1,0:T(8,128)(2,1)}) fusion(bf16[4096,256]{1,0:T(8,128)(2,1)} %all-gather.4.cloned.1.call-done), kind=kLoop, calls=%fused_computation.72 | loop fusion | bytes 4194304 | tf_op jit(solution)/shard_map/slice | solution.py:99
  101.2 1.5 copy.53
  102.7 2.3 copy.52
  105.0 3.1 %bitcast_reduce_fusion = (f32[128,2,3]{0,2,1:T(4,128)S(1)}, f32[2,4096,128,3]{2,1,3,0:T(8,128)S(1)}) fusion(bf16[4096,2,64,1]{0,2,3,1:T(8,128)(2,1)} %bitcast.80, bf16[128,2,3,32]{0,3,2,1:T(8,128)(2,1)S(1)} %bitcast.88, bf16[128,2,3,32]{0,3,2,1:T(8,128)(2,1)S(1)} %bitcast.86), kind=kOutput, calls=%fused_computation.1 | convolution fusion | flops 409140480 | bytes 13732864 | tf_op jit(solution)/shard_map/tkgd,pkd->tkgp/dot_general | solution.py:105
  108.0 2.0 fusion.1
  110.1 2.3 fusion.10
  112.6 1.3 fusion.42
  114.0 0.5 all-gather.6.cloned.1.call-update
  114.8 0.7 select_reduce_fusion.1
  115.6 0.2 fusion.19
  115.8 22.7 %reduce-scatter.2.cloned.1.call-done = f32[32,1536]{1,0:T(8,128)} async-done(((f32[128,1536]{1,0:T(8,128)}), f32[32,1536]{1,0:T(8,128)}) %reduce-scatter.2.cloned.1.call-update) | async-done | bytes 196624 | tf_op jit(solution)/shard_map/reduce_scatter | solution.py:126
  138.5 1.1 multiply_reduce_fusion
  139.6 2.7 convolution_convert_fusion
  142.3 12.8 %all-to-all-start = ((bf16[32,16,1536]{2,1,0:T(8,128)(2,1)}), bf16[32,16,1536]{2,1,0:T(8,128)(2,1)S(1)}, u32[]{:S(2)}, u32[]{:S(2)}) async-start(bf16[32,16,1536]{2,1,0:T(8,128)(2,1)} %bitcast.21), calls=%async_computation.1 | async-start | bytes 3145728 | tf_op jit(solution)/shard_map/all_to_all | solution.py:153
  155.3 0.4 all-gather.8.cloned.1.call-update
  155.7 14.9 %all-gather.6.cloned.1.call-done = bf16[4,1536,256]{2,1,0:T(8,128)(2,1)} async-done(((bf16[1,1536,256]{2,1,0:T(8,128)(2,1)}), bf16[4,1536,256]{2,1,0:T(8,128)(2,1)}) %all-gather.6.cloned.1.call-update) | async-done | bytes 3145744 | tf_op jit(solution)/shard_map/all_gather | solution.py:155
  170.5 26.1 %all-to-all-done = bf16[32,16,1536]{2,1,0:T(8,128)(2,1)S(1)} async-done(((bf16[32,16,1536]{2,1,0:T(8,128)(2,1)}), bf16[32,16,1536]{2,1,0:T(8,128)(2,1)S(1)}, u32[]{:S(2)}, u32[]{:S(2)}) %all-to-all-start) | async-done | bytes 1572896 | tf_op jit(solution)/shard_map/all_to_all | solution.py:153
  196.7 5.1 %convolution_bitcast_fusion = f32[4,512,256]{2,1,0:T(8,128)} fusion(bf16[512,1536,1]{1,0,2:T(8,128)(2,1)S(1)} %bitcast.81, bf16[4,1536,256]{2,1,0:T(8,128)(2,1)} %all-gather.6.cloned.1.call-done), kind=kOutput, calls=%fused_computation.8 | convolution fusion | flops 1610612736 | bytes 6815744 | tf_op jit(solution)/shard_map/rd,pdf->prf/dot_general | solution.py:157
  201.8 3.8 %all-gather.8.cloned.1.call-done = bf16[4,128,1536]{2,1,0:T(8,128)(2,1)} async-done(((bf16[1,128,1536]{2,1,0:T(8,128)(2,1)}), bf16[4,128,1536]{2,1,0:T(8,128)(2,1)}) %all-gather.8.cloned.1.call-update) | async-done | bytes 1572880 | tf_op jit(solution)/shard_map/all_gather | solution.py:156
  205.5 5.4 %convert_reduce_fusion = bf16[512,1536]{1,0:T(8,128)(2,1)} fusion(bf16[4,128,1536]{2,1,0:T(8,128)(2,1)} %all-gather.8.cloned.1.call-done, f32[4,512,256]{2,1,0:T(8,128)} %convolution_bitcast_fusion), kind=kOutput, calls=%fused_computation.5 | convolution fusion | flops 812384256 | bytes 5242880 | tf_op jit(solution)/shard_map/prf,pfd->prd/dot_general | solution.py:159
  210.9 12.0 %all-to-all-start.1 = ((bf16[32,16,1536]{2,1,0:T(8,128)(2,1)}), bf16[32,16,1536]{2,1,0:T(8,128)(2,1)S(1)}, u32[]{:S(2)}, u32[]{:S(2)}) async-start(bf16[32,16,1536]{2,1,0:T(8,128)(2,1)} %bitcast.82), calls=%async_computation.2 | async-start | bytes 3145728 | tf_op jit(solution)/shard_map/all_to_all | solution.py:163
  223.2 47.9 %all-to-all-done.1 = bf16[32,16,1536]{2,1,0:T(8,128)(2,1)S(1)} async-done(((bf16[32,16,1536]{2,1,0:T(8,128)(2,1)}), bf16[32,16,1536]{2,1,0:T(8,128)(2,1)S(1)}, u32[]{:S(2)}, u32[]{:S(2)}) %all-to-all-start.1) | async-done | bytes 1572896 | tf_op jit(solution)/shard_map/all_to_all | solution.py:163
  271.1 1.5 add_convert_fusion
  (38 shorter events, 1.6 us)
Async XLA Ops:
  8.0 104.6 %copy-start = (bf16[384,1536]{1,0:T(8,128)(2,1)S(1)}, bf16[384,1536]{1,0:T(8,128)(2,1)}, u32[]{:S(2)}) copy-start(bf16[384,1536]{1,0:T(8,128)(2,1)} %param.16) | copy-start | bytes 3538948
  8.0 90.2 %all-gather.4.cloned.1.call-start = ((), (), s32[]{:S(2)}) async-start(), calls=%async_computation.3 | async-start | bytes 2113536 | tf_op jit(solution)/shard_map/all_gather | solution.py:97
  9.5 129.0 %reduce-scatter.2.cloned.1.call-start = ((), (), s32[]{:S(2)}) async-start(), calls=%async_computation.4 | async-start | bytes 983040 | tf_op jit(solution)/shard_map/reduce_scatter | solution.py:126
  11.5 4.9 %copy-start.1 = (bf16[128,1536]{1,0:T(8,128)(2,1)S(1)}, bf16[128,1536]{1,0:T(8,128)(2,1)}, u32[]{:S(2)}) copy-start(bf16[128,1536]{1,0:T(8,128)(2,1)} %param.12) | copy-start | bytes 1179652
  11.5 4.9 %copy-start.3 = (bf16[1536,128]{1,0:T(8,128)(2,1)S(1)}, bf16[1536,128]{1,0:T(8,128)(2,1)}, u32[]{:S(2)}) copy-start(bf16[1536,128]{1,0:T(8,128)(2,1)} %param.15) | copy-start | bytes 1179652
  112.4 2.1 copy-start.4
  113.9 56.6 %all-gather.6.cloned.1.call-start = ((), (), s32[]{:S(2)}) async-start(), calls=%async_computation.5 | async-start | bytes 3932160 | tf_op jit(solution)/shard_map/all_gather | solution.py:155
  142.3 54.4 %all-to-all-start = ((bf16[32,16,1536]{2,1,0:T(8,128)(2,1)}), bf16[32,16,1536]{2,1,0:T(8,128)(2,1)S(1)}, u32[]{:S(2)}, u32[]{:S(2)}) async-start(bf16[32,16,1536]{2,1,0:T(8,128)(2,1)} %bitcast.21), calls=%async_computation.1 | async-start | bytes 3145728 | tf_op jit(solution)/shard_map/all_to_all | solution.py:153
  155.1 50.4 %all-gather.8.cloned.1.call-start = ((), (), s32[]{:S(2)}) async-start(), calls=%async_computation.6 | async-start | bytes 1966080 | tf_op jit(solution)/shard_map/all_gather | solution.py:156
  210.9 12.0 %copy-start.5 = (f32[32,8]{0,1:T(8,128)S(1)}, f32[32,8]{0,1:T(8,128)}, u32[]{:S(2)}) copy-start(f32[32,8]{0,1:T(8,128)} %param.21) | copy-start | bytes 3076
  210.9 60.3 %copy-start.2 = (f32[32,1536]{1,0:T(8,128)S(1)}, f32[32,1536]{1,0:T(8,128)}, u32[]{:S(2)}) copy-start(f32[32,1536]{1,0:T(8,128)} %reduce-scatter.2.cloned.1.call-done) | copy-start | bytes 589828
  210.9 60.3 %all-to-all-start.1 = ((bf16[32,16,1536]{2,1,0:T(8,128)(2,1)}), bf16[32,16,1536]{2,1,0:T(8,128)(2,1)S(1)}, u32[]{:S(2)}, u32[]{:S(2)}) async-start(bf16[32,16,1536]{2,1,0:T(8,128)(2,1)} %bitcast.82), calls=%async_computation.2 | async-start | bytes 3145728 | tf_op jit(solution)/shard_map/all_to_all | solution.py:163
Sparse Core Ops, SparseCore 0:
  12.5 85.6 all-gather.3
  114.0 24.4 reduce-scatter.1
Sparse Core Ops, SparseCore 1:
  116.5 54.0 all-gather.5
  172.5 32.9 all-gather.7
where the time goes:
time: 281 us; the launch traced here: 280 us
  waiting for transfers between devices  198 us (70%)
  matrix products  25.6 us (9%)
  starting transfers between devices  25.1 us (9%)
  between operations  15.7 us (6%)
  other arithmetic  8.96 us (3%)
  local copies, waits for them, and re-layouts  7.04 us (3%)
    all_gather x1, waiting for transfers between devices, body(): whole_both = lax.all_gather(prefix_both, SEQ, axis=0, tiled=True)  81.4 us
    all_to_all x1, waiting for transfers between devices, body(): lax.all_to_all(part_total.reshape(experts, capacity, column_list), EXPERT...  47.9 us
    all_to_all x1, waiting for transfers between devices, body(): lax.all_to_all(outgoing, EXPERT_AXES, split_axis=0, concat_axis=0, tiled=...  26.1 us
    reduce_scatter x1, waiting for transfers between devices, body(): lax.psum_scatter(jnp.dot(attended, w_out, preferred_element_type=jnp.floa...  22.7 us
    all_gather x1, waiting for transfers between devices, body(): full_in = lax.all_gather(expert_in, PART_AXES, axis=0, tiled=True)  14.9 us
    all_to_all x1, starting transfers between devices, body(): lax.all_to_all(outgoing, EXPERT_AXES, split_axis=0, concat_axis=0, tiled=...  12.8 us
    all_to_all x1, starting transfers between devices, body(): lax.all_to_all(part_total.reshape(experts, capacity, column_list), EXPERT...  12 us
  transfers between devices with their start and end apart: 6, of which 6 were waited for; matrix products, arithmetic and copies ran while one was open for 6% of the time, Pallas kernels for 0%

commit v1 on v0

--- a/solution.py
+++ b/solution.py
@@ -152,7 +152,15 @@
     outgoing = gathered.reshape(experts, capacity, column_list)
     incoming = lax.all_to_all(outgoing, EXPERT_AXES, split_axis=0, concat_axis=0, tiled=True)
     incoming = incoming.reshape(experts * capacity, column_list)
-    full_in = lax.all_gather(expert_in, PART_AXES, axis=0, tiled=True)
+    full_in = jnp.concatenate(
+        lax.all_to_all(
+            jnp.stack([expert_in for _ in range(lax.axis_size(PART_AXES))]),
+            axis_name=PART_AXES,
+            split_axis=0,
+            concat_axis=0,
+        ),
+        axis=0,
+    )
     full_out = lax.all_gather(expert_out, PART_AXES, axis=0, tiled=True)
     gate_up = jnp.einsum("rd,pdf->prf", incoming, full_in, preferred_element_type=jnp.float32)
     activated = (jax.nn.silu(gate_up[..., :ff_part]) * gate_up[..., ff_part:]).astype(jnp.bfloat16)

time: 281 us -> 275 us (0.979)
  the two profiles are of different devices: /device:TPU:84 before, /device:TPU:24 now
where the time goes in v1:
time: 275 us
  waiting for transfers between devices  190 us (69%)
  starting transfers between devices  29.3 us (11%)
  matrix products  23.1 us (8%)
  between operations  15.7 us (6%)
  local copies, waits for them, and re-layouts  10.2 us (4%)
  other arithmetic  6.49 us (2%)
    all_gather x1, waiting for transfers between devices, body(): whole_both = lax.all_gather(prefix_both, SEQ, axis=0, tiled=True)  79.5 us
    all_to_all x1, waiting for transfers between devices, body(): lax.all_to_all(part_total.reshape(experts, capacity, column_list), EXPERT...  43.1 us
    all_to_all x1, waiting for transfers between devices, body(): lax.all_to_all(outgoing, EXPERT_AXES, split_axis=0, concat_axis=0, tiled=...  43 us
    reduce_scatter x1, waiting for transfers between devices, body(): lax.psum_scatter(jnp.dot(attended, w_out, preferred_element_type=jnp.floa...  24 us
    all_to_all x1, starting transfers between devices, body(): lax.all_to_all(outgoing, EXPERT_AXES, split_axis=0, concat_axis=0, tiled=...  12.1 us
    all_to_all x1, starting transfers between devices, body(): lax.all_to_all(part_total.reshape(experts, capacity, column_list), EXPERT...  11.8 us
  transfers between devices with their start and end apart: 6, of which 4 were waited for; matrix products, arithmetic and copies ran while one was open for 11% of the time, Pallas kernels for 0%

profile of v1, /device:TPU:24, one launch (start us, length us, event | category | flops | bytes accessed | tf_op | source)
XLA Modules:
  0.0 274.8 jit_solution(11552152033732922873)
XLA Ops:
  8.1 1.4 pad_maximum_fusion.3
  9.5 3.0 %stack.2 = bf16[4,1,1536,256]{3,2,1,0:T(8,128)(2,1)} broadcast(bf16[1536,256]{1,0:T(8,128)(2,1)} %bitcast.89), dimensions={2,3} | broadcast | bytes 3932160 | tf_op jit(solution)/shard_map/stack | solution.py:157
  12.5 5.2 %all-to-all-start.1 = ((bf16[4,1,1536,256]{3,2,1,0:T(8,128)(2,1)}), bf16[4,1,1536,256]{3,2,1,0:T(8,128)(2,1)}, u32[]{:S(2)}, u32[]{:S(2)}) async-start(bf16[4,1,1536,256]{3,2,1,0:T(8,128)(2,1)} %stack.2), calls=%async_computation.2 | async-start | bytes 6291456 | tf_op jit(solution)/shard_map/all_to_all | solution.py:156
  17.9 0.2 fusion.20
  18.3 0.4 fusion.42
  18.7 0.6 fusion.40
  19.3 0.3 fusion.46
  19.7 0.3 convolution_convert_fusion.1
  20.1 79.5 %all-gather.3.cloned.1.call-done = bf16[4096,256]{1,0:T(8,128)(2,1)} async-done(((bf16[32,256]{1,0:T(8,128)(2,1)}), bf16[4096,256]{1,0:T(8,128)(2,1)}) %all-gather.3.cloned.1.call-update) | async-done | bytes 2097168 | tf_op jit(solution)/shard_map/all_gather | solution.py:97
  99.6 3.1 %fusion.45 = (bf16[4096,128]{1,0:T(8,128)(2,1)}, bf16[4096,128]{1,0:T(8,128)(2,1)}) fusion(bf16[4096,256]{1,0:T(8,128)(2,1)} %all-gather.3.cloned.1.call-done), kind=kLoop, calls=%fused_computation.74 | loop fusion | bytes 4194304 | tf_op jit(solution)/shard_map/slice | solution.py:99
  102.6 1.5 copy.53
  104.1 2.3 copy.52
  106.4 3.1 %bitcast_reduce_fusion = (f32[128,2,3]{0,2,1:T(4,128)S(1)}, f32[2,4096,128,3]{2,1,3,0:T(8,128)S(1)}) fusion(bf16[4096,2,64,1]{0,2,3,1:T(8,128)(2,1)} %bitcast.85, bf16[128,2,3,32]{0,3,2,1:T(8,128)(2,1)S(1)} %bitcast.94, bf16[128,2,3,32]{0,3,2,1:T(8,128)(2,1)S(1)} %bitcast.92), kind=kOutput, calls=%fused_computation.1 | convolution fusion | flops 409140480 | bytes 13732864 | tf_op jit(solution)/shard_map/tkgd,pkd->tkgp/dot_general | solution.py:105
  109.5 2.0 fusion.1
  111.6 2.3 fusion.15
  113.8 0.2 fusion.18
  114.1 1.3 fusion.47
  115.6 0.7 select_reduce_fusion.1
  116.5 0.2 fusion.24
  116.7 24.0 %reduce-scatter.2.cloned.1.call-done = f32[32,1536]{1,0:T(8,128)} async-done(((f32[128,1536]{1,0:T(8,128)}), f32[32,1536]{1,0:T(8,128)}) %reduce-scatter.2.cloned.1.call-update) | async-done | bytes 196624 | tf_op jit(solution)/shard_map/reduce_scatter | solution.py:126
  140.7 1.1 multiply_reduce_fusion
  141.8 2.7 convolution_convert_fusion
  144.5 12.1 %all-to-all-start = ((bf16[32,16,1536]{2,1,0:T(8,128)(2,1)}), bf16[32,16,1536]{2,1,0:T(8,128)(2,1)S(1)}, u32[]{:S(2)}, u32[]{:S(2)}) async-start(bf16[32,16,1536]{2,1,0:T(8,128)(2,1)} %bitcast.21), calls=%async_computation.1 | async-start | bytes 3145728 | tf_op jit(solution)/shard_map/all_to_all | solution.py:153
  156.6 0.2 all-gather.5.cloned.1.call-start
  156.9 0.3 all-gather.5.cloned.1.call-update
  157.2 43.0 %all-to-all-done = bf16[32,16,1536]{2,1,0:T(8,128)(2,1)S(1)} async-done(((bf16[32,16,1536]{2,1,0:T(8,128)(2,1)}), bf16[32,16,1536]{2,1,0:T(8,128)(2,1)S(1)}, u32[]{:S(2)}, u32[]{:S(2)}) %all-to-all-start) | async-done | bytes 1572896 | tf_op jit(solution)/shard_map/all_to_all | solution.py:153
  200.2 5.0 %fusion.7 = f32[4,512,256]{2,1,0:T(8,128)} fusion(bf16[512,1536,1]{1,0,2:T(8,128)(2,1)S(1)} %bitcast.86, bf16[4,1,1536,256]{3,2,1,0:T(8,128)(2,1)} %all-to-all-done.1), kind=kOutput, calls=%fused_computation.10 | convolution fusion | flops 1610612736 | bytes 6815744 | tf_op jit(solution)/shard_map/rd,pdf->prf/dot_general | solution.py:165
  205.3 5.4 %convert_reduce_fusion = bf16[512,1536]{1,0:T(8,128)(2,1)} fusion(bf16[4,128,1536]{2,1,0:T(8,128)(2,1)} %all-gather.5.cloned.1.call-done, f32[4,512,256]{2,1,0:T(8,128)} %fusion.7), kind=kOutput, calls=%fused_computation.5 | convolution fusion | flops 812384256 | bytes 5242880 | tf_op jit(solution)/shard_map/prf,pfd->prd/dot_general | solution.py:167
  210.7 11.8 %all-to-all-start.2 = ((bf16[32,16,1536]{2,1,0:T(8,128)(2,1)}), bf16[32,16,1536]{2,1,0:T(8,128)(2,1)S(1)}, u32[]{:S(2)}, u32[]{:S(2)}) async-start(bf16[32,16,1536]{2,1,0:T(8,128)(2,1)} %bitcast.87), calls=%async_computation.3 | async-start | bytes 3145728 | tf_op jit(solution)/shard_map/all_to_all | solution.py:171
  222.5 0.2 select_reduce_fusion
  222.7 43.1 %all-to-all-done.2 = bf16[32,16,1536]{2,1,0:T(8,128)(2,1)S(1)} async-done(((bf16[32,16,1536]{2,1,0:T(8,128)(2,1)}), bf16[32,16,1536]{2,1,0:T(8,128)(2,1)S(1)}, u32[]{:S(2)}, u32[]{:S(2)}) %all-to-all-start.2) | async-done | bytes 1572896 | tf_op jit(solution)/shard_map/all_to_all | solution.py:171
  265.9 1.5 add_convert_fusion
  (44 shorter events, 1.1 us)
Async XLA Ops:
  8.0 106.1 %copy-start = (bf16[384,1536]{1,0:T(8,128)(2,1)S(1)}, bf16[384,1536]{1,0:T(8,128)(2,1)}, u32[]{:S(2)}) copy-start(bf16[384,1536]{1,0:T(8,128)(2,1)} %param.16) | copy-start | bytes 3538948
  8.0 91.6 %all-gather.3.cloned.1.call-start = ((), (), s32[]{:S(2)}) async-start(), calls=%async_computation.4 | async-start | bytes 2113536 | tf_op jit(solution)/shard_map/all_gather | solution.py:97
  12.5 5.2 %copy-start.8 = (s32[1,128]{1,0:T(1,128)S(1)}, s32[1,128]{1,0:T(1,128)}, u32[]{:S(2)}) copy-start(s32[1,128]{1,0:T(1,128)} %param.19) | copy-start | bytes 1540
  12.5 5.3 %copy-start.1 = (bf16[128,1536]{1,0:T(8,128)(2,1)S(1)}, bf16[128,1536]{1,0:T(8,128)(2,1)}, u32[]{:S(2)}) copy-start(bf16[128,1536]{1,0:T(8,128)(2,1)} %param.12) | copy-start | bytes 1179652
  12.5 5.8 %copy-start.4 = (bf16[1536,128]{1,0:T(8,128)(2,1)S(1)}, bf16[1536,128]{1,0:T(8,128)(2,1)}, u32[]{:S(2)}) copy-start(bf16[1536,128]{1,0:T(8,128)(2,1)} %param.14) | copy-start | bytes 1179652
  12.5 6.1 %copy-start.3 = (bf16[1536,384]{1,0:T(8,128)(2,1)S(1)}, bf16[1536,384]{1,0:T(8,128)(2,1)}, u32[]{:S(2)}) copy-start(bf16[1536,384]{1,0:T(8,128)(2,1)} %param.13) | copy-start | bytes 3538948
  12.5 132.0 %all-to-all-start.1 = ((bf16[4,1,1536,256]{3,2,1,0:T(8,128)(2,1)}), bf16[4,1,1536,256]{3,2,1,0:T(8,128)(2,1)}, u32[]{:S(2)}, u32[]{:S(2)}) async-start(bf16[4,1,1536,256]{3,2,1,0:T(8,128)(2,1)} %stack.2), calls=%async_computation.2 | async-start | bytes 6291456 | tf_op jit(solution)/shard_map/all_to_all | solution.py:156
  17.7 123.0 %reduce-scatter.2.cloned.1.call-start = ((), (), s32[]{:S(2)}) async-start(), calls=%async_computation.5 | async-start | bytes 983040 | tf_op jit(solution)/shard_map/reduce_scatter | solution.py:126
  18.0 1.7 copy-start.5
  113.8 1.5 copy-start.6
  144.5 55.7 %all-to-all-start = ((bf16[32,16,1536]{2,1,0:T(8,128)(2,1)}), bf16[32,16,1536]{2,1,0:T(8,128)(2,1)S(1)}, u32[]{:S(2)}, u32[]{:S(2)}) async-start(bf16[32,16,1536]{2,1,0:T(8,128)(2,1)} %bitcast.21), calls=%async_computation.1 | async-start | bytes 3145728 | tf_op jit(solution)/shard_map/all_to_all | solution.py:153
  156.6 48.7 %all-gather.5.cloned.1.call-start = ((), (), s32[]{:S(2)}) async-start(), calls=%async_computation.6 | async-start | bytes 1966080 | tf_op jit(solution)/shard_map/all_gather | solution.py:164
  210.7 11.8 %copy-start.7 = (f32[32,8]{0,1:T(8,128)S(1)}, f32[32,8]{0,1:T(8,128)}, u32[]{:S(2)}) copy-start(f32[32,8]{0,1:T(8,128)} %param.21) | copy-start | bytes 3076
  210.7 55.2 %copy-start.2 = (f32[32,1536]{1,0:T(8,128)S(1)}, f32[32,1536]{1,0:T(8,128)}, u32[]{:S(2)}) copy-start(f32[32,1536]{1,0:T(8,128)} %reduce-scatter.2.cloned.1.call-done) | copy-start | bytes 589828
  210.7 55.2 %all-to-all-start.2 = ((bf16[32,16,1536]{2,1,0:T(8,128)(2,1)}), bf16[32,16,1536]{2,1,0:T(8,128)(2,1)S(1)}, u32[]{:S(2)}, u32[]{:S(2)}) async-start(bf16[32,16,1536]{2,1,0:T(8,128)(2,1)} %bitcast.87), calls=%async_computation.3 | async-start | bytes 3145728 | tf_op jit(solution)/shard_map/all_to_all | solution.py:171
Sparse Core Ops, SparseCore 0:
  12.5 87.0 all-gather.2
  115.5 25.1 reduce-scatter.1
Sparse Core Ops, SparseCore 1:
  159.2 42.3 all-gather.4
